TPU v7x, 32 devices: a whole 2x2x4 slice. The times are simulated.
32 devices in a mesh: groups: 2 (over y), ctx: 4 (over z), chan: 2 (over x), sub: 2 (over core).
Axes of the slice: x: 2, y: 2, z: 4, core: 2. Of those that a mesh axis runs over, the one named last changes fastest.
Arguments:
- queries: float32 [2048, 8192], P(('groups', 'ctx'), ('chan', 'sub')), parts along dimension 0, may hold values from -6 to 6
- key_in: float32 [2048, 8192], P(('groups', 'ctx'), ('chan', 'sub')), parts along dimension 0, may hold values from -6 to 6
- values_in: float32 [2048, 8192], P(('groups', 'ctx'), ('chan', 'sub')), parts along dimension 0, may hold values from -6 to 6
- skip_gain: float32 [8192], P(('chan', 'sub')), may hold values from 0.5 to 1.5
- filter_tap_bank: float32 [16, 256, 512], P(('ctx', 'sub'), None, 'chan'), may hold values from -0.1875 to 0.1875
- lag_slot: int32 [4], replicated, may hold values from 0 to 15, as said below
Outputs:
- gated_output: float32 [2048, 8192], P(('groups', 'ctx'), ('chan', 'sub')), parts along dimension 0
There are 2 independent parts, one for each index of `groups`. A program takes and returns all parts, laid end to end along the dimension named above; an argument that names none is the same for every part. Nothing has to cross between parts.
Inputs may be any that keep to these rules, and one draw needn't show every extreme that they name: `lag_slot`: the 4 entries are distinct slots; entry k names the slot that holds lags k * 256 to (k + 1) * 256 - 1.
All inputs are finite; a program needn't handle non-finite values.
Results may differ from a plain program's by a relative error of at most 0.00005.
Values sent between devices are 32-bit elements; how exact they have to be, the bound alone decides.
No kernel may reach another device: no remote copies, remote signals or barrier semaphores. Data moves between devices by JAX's collectives and lax.ppermute only.
A program may use at most 128 MiB of HBM per device.

v0:
```python
import jax
import jax.numpy as jnp
from jax import lax
from jax.sharding import PartitionSpec as P

HIGHEST = lax.Precision.HIGHEST
DATA_PRECISION = lax.Precision.HIGH
CHUNKS = 4


def from_root(block, axis, owner):
    block = jnp.where(lax.axis_index(axis) == owner, block, jnp.zeros_like(block))
    return lax.psum(block, axis)


def tables(length):
    freq_rows = lax.broadcasted_iota(jnp.int32, (length, length), 0)
    place_cols = lax.broadcasted_iota(jnp.int32, (length, length), 1)
    angle = jnp.pi * (freq_rows * place_cols % (2 * length)).astype(jnp.float32) / length
    parity = 1.0 - 2.0 * (place_cols % 2).astype(jnp.float32)
    fwd_real = jnp.cos(angle)
    fwd_imag = jnp.where(freq_rows == 0, parity, -jnp.sin(angle))
    out_place = freq_rows + length
    back_angle = jnp.pi * (place_cols * out_place % (2 * length)).astype(jnp.float32) / length
    out_parity = 1.0 - 2.0 * (out_place % 2).astype(jnp.float32)
    inv_real = jnp.where(place_cols == 0, 1.0, 2.0 * jnp.cos(back_angle)) / (2 * length)
    inv_imag = jnp.where(place_cols == 0, out_parity, -2.0 * jnp.sin(back_angle)) / (2 * length)
    return (fwd_real, fwd_imag, inv_real, inv_imag)


def transform(block, fwd_real, fwd_imag, precision=DATA_PRECISION):
    return jnp.stack(
        [jnp.dot(fwd_real, block, precision=precision), jnp.dot(fwd_imag, block, precision=precision)]
    )


def inverse(total, inv_real, inv_imag):
    return jnp.dot(inv_real, total[0], precision=DATA_PRECISION) + jnp.dot(
        inv_imag, total[1], precision=DATA_PRECISION
    )


def apply_filter(spectrum, filt):
    length = spectrum.shape[1]
    chan_width = spectrum.shape[2]
    group_dev = filt.shape[2]
    a_real = spectrum[0].reshape(length, chan_width // group_dev, group_dev)
    a_imag = spectrum[1].reshape(length, chan_width // group_dev, group_dev)
    e_real = filt[0][:, None, :]
    e_imag = filt[1][:, None, :]
    first_row = lax.broadcasted_iota(jnp.int32, (length, 1, 1), 0) == 0
    prod_real = jnp.where(first_row, a_real * e_real, a_real * e_real - a_imag * e_imag)
    prod_imag = jnp.where(first_row, a_imag * e_imag, a_real * e_imag + a_imag * e_real)
    return jnp.stack([prod_real.reshape(length, chan_width), prod_imag.reshape(length, chan_width)])


def filtered_sum(specs, filters):
    total = apply_filter(specs[0], filters[0])
    for spec, filt in zip(specs[1:], filters[1:]):
        total = total + apply_filter(spec, filt)
    return total


def body(queries, key_in, values_in, skip_gain, filter_tap_bank, lag_slot):
    length, chan_width = key_in.shape
    slots_dev = filter_tap_bank.shape[0]
    cycle_steps = lag_slot.shape[0]
    group_dev = filter_tap_bank.shape[2] // lax.axis_size("sub")
    n_ctx = lax.axis_size("ctx")
    sub_index = lax.axis_index("sub")
    mixed_input = key_in * values_in
    fwd_real, fwd_imag, inv_real, inv_imag = lax.optimization_barrier(tables(length))
    members = chan_width // group_dev
    member_major = (
        mixed_input.reshape(length, group_dev, members).transpose(0, 2, 1).reshape(length, chan_width)
    )
    n_sub = lax.axis_size("sub")
    received = []
    for offset in range(n_sub):
        wanted = lax.dynamic_slice_in_dim(
            filter_tap_bank, ((sub_index + offset) % n_sub) * group_dev, group_dev, 2
        )
        if offset:
            wanted = lax.ppermute(
                wanted, "sub", [(i, (i + offset) % n_sub) for i in range(n_sub)]
            )
        received.append(wanted)
    received = jnp.stack(received)
    pieces = []
    for cycle_step in range(cycle_steps):
        slot_index = lag_slot[cycle_step]
        owner = slot_index // slots_dev
        source = (sub_index - owner % n_sub) % n_sub
        held_piece = received[source, slot_index % slots_dev]
        pieces.append(from_root(held_piece, "ctx", owner // n_sub))
    filter_taps = jnp.concatenate(pieces, axis=1)
    filter_spec = transform(filter_taps, fwd_real, fwd_imag, HIGHEST)
    row_sign = (
        1.0 - 2.0 * (lax.broadcasted_iota(jnp.int32, (length, 1), 0) % 2).astype(jnp.float32)
    )[None]
    segment_spec = [
        filter_spec[:, :, cycle_step * group_dev : (cycle_step + 1) * group_dev]
        for cycle_step in range(cycle_steps)
    ]
    effective = [row_sign * segment_spec[0]]
    for cycle_step in range(1, cycle_steps):
        effective.append(segment_spec[cycle_step - 1] + row_sign * segment_spec[cycle_step])
    effective.append(segment_spec[cycle_steps - 1])

    last_raw = max(n_ctx - 2, 0)
    raw_rounds = min(cycle_steps, last_raw)
    part_terms = min(cycle_steps, raw_rounds + 1)
    chunks = CHUNKS if members % CHUNKS == 0 else 1
    chunk_w = chan_width // chunks
    outs = []
    last_round = None
    partial = None
    sent = None
    for chunk in range(chunks):
        cols = slice(chunk * chunk_w, (chunk + 1) * chunk_w)
        filters = effective
        moving = member_major[:, cols]
        blocks = [moving]
        for step in range(1, raw_rounds + 1):
            route = [(k, k + 1) for k in range(step - 1, last_raw)]
            if step == raw_rounds and step > 1 and last_round is not None:
                moving, _ = lax.optimization_barrier((moving, last_round))
            moving = lax.ppermute(moving, "ctx", route)
            if step == raw_rounds and step > 1 and partial is not None:
                moving, _ = lax.optimization_barrier((moving, partial))
            blocks.append(moving)
        if raw_rounds > 1:
            last_round = blocks[-1]
        specs = [transform(b, fwd_real, fwd_imag) for b in blocks]
        conv_out = inverse(filtered_sum(specs, filters), inv_real, inv_imag)
        if n_ctx >= 2:
            part_specs = specs[:part_terms]
            if sent is not None:
                part_specs, _ = lax.optimization_barrier((part_specs, sent))
            partial = inverse(
                filtered_sum(part_specs, filters[1 : part_terms + 1]), inv_real, inv_imag
            )
            sent = lax.ppermute(partial, "ctx", [(last_raw, last_raw + 1)])
            conv_out = conv_out + sent
        outs.append(conv_out)
    conv_all = jnp.concatenate(outs, axis=1) if chunks > 1 else outs[0]
    conv_all = conv_all.reshape(length, members, group_dev).transpose(0, 2, 1).reshape(length, chan_width)
    return queries * (conv_all + skip_gain[None, :] * mixed_input)


def solution(mesh):
    in_specs = (
        P(("groups", "ctx"), ("chan", "sub")),
        P(("groups", "ctx"), ("chan", "sub")),
        P(("groups", "ctx"), ("chan", "sub")),
        P(("chan", "sub")),
        P(("ctx", "sub"), None, "chan"),
        P(),
    )
    out_specs = P(("groups", "ctx"), ("chan", "sub"))
    return jax.shard_map(body, mesh=mesh, in_specs=in_specs, out_specs=out_specs, check_vma=False)
```

profile of v0, /device:TPU:24, one launch (start us, length us, event | category | flops | bytes accessed | tf_op | source)
XLA Modules:
  0.0 214.0 jit_solution(7858944070214772802)
XLA Ops:
  6.5 1.8 constant_dynamic-slice_fusion
  8.3 1.9 copy.8
  10.3 2.9 %copy.9 = f32[256,2048]{0,1:T(8,128)} copy(f32[256,2048]{1,0:T(8,128)} %param.8) | data formatting | bytes 4194304 | tf_op args[2]
  13.1 1.9 mul.501
  15.0 1.2 copy.10
  16.3 1.4 fusion.129
  17.7 1.5 collective-permute-start.1
  19.2 1.5 collective-permute-start.4
  20.6 1.5 collective-permute-start.7
  22.1 2.0 collective-permute-start.10
  25.1 2.1 %select_multiply_fusion = (f32[256,256]{1,0:T(8,128)S(1)}, f32[256,256]{1,0:T(8,128)S(1)}, f32[256,256]{1,0:T(8,128)S(1)}) fusion(s32[256]{0:T(256)S(1)} %get-tuple-element.163, s32[256]{0:T(256)S(1)} %get-tuple-element.164, s32[256]{0:T(256)S(1)} %get-tuple-element.167, pred[256]{0:T(512)(128)(4,1)S(1)} %get-tuple-element.165, ...), kind=kLoop, calls=%fused_computation.263 | loop fusion | flops 2883584 | bytes 792320 | tf_op jit(solution)/shard_map/div | solution.py:27
  27.2 1.2 fusion.125
  45.3 2.9 %copy.12 = f32[256,2048]{0,1:T(8,128)} copy(f32[256,2048]{1,0:T(8,128)} %param.6) | data formatting | bytes 4194304 | tf_op args[0]
  48.2 1.3 fusion.127
  49.4 1.7 fusion.100
  51.1 1.6 fusion.109
  52.7 1.5 fusion.134
  54.2 1.7 fusion.135
  55.9 1.7 fusion.138
  57.6 1.7 fusion.139
  59.2 1.2 pad_maximum_fusion.1
  60.4 1.5 fusion.142
  61.9 1.7 fusion.143
  63.6 1.6 collective-permute-start.2
  67.4 2.3 %fusion.131 = f32[256,512]{1,0:T(8,128)} fusion(f32[256,256]{1,0:T(8,128)S(1)} %fusion.110, f32[256,512]{0,1:T(8,128)} %collective-permute-done.1), kind=kOutput, calls=%fused_computation.328 | convolution fusion | flops 201326592 | bytes 1310720 | tf_op jit(solution)/shard_map/dot_general | solution.py:33
  69.7 29.0 %all-reduce.3.cloned.1.call-done = (f32[256,128]{1,0:T(8,128)}, f32[256,128]{1,0:T(8,128)}, f32[256,128]{1,0:T(8,128)}, f32[256,128]{1,0:T(8,128)}) async-done(((f32[256,128]{1,0:T(8,128)}, f32[256,128]{1,0:T(8,128)}, f32[256,128]{1,0:T(8,128)}, f32[256,128]{1,0:T(8,128)}), (f32[256,128]{1,0:T(8,128)}, f32[256,128]{1,0:T(8,128)}, f32[256,128]{1,0:T(8,128)}, ...) | async-done | bytes 524304 | tf_op jit(solution)/shard_map/psum | solution.py:13
  109.7 1.3 mul.579
  112.9 2.0 mul.583
  115.8 2.1 mul.585
  118.7 1.5 fusion.132
  120.3 1.6 fusion.133
  124.0 3.6 %fusion.15 = (f32[1,256,512]{2,1,0:T(8,128)S(1)}, f32[1,256,512]{2,1,0:T(8,128)S(1)}, f32[1,256,512]{2,1,0:T(8,128)S(1)}, f32[1,256,512]{2,1,0:T(8,128)S(1)}, f3...) fusion(f32[256,512]{1,0:T(8,128)S(1)} %fusion.132, ...), kind=kOutput, calls=%fused_computation.82 | convolution fusion | flops 209715200 | bytes 18088192 | tf_op jit(solution)/shard_map/dot_general | solution.py:33
  128.8 1.3 collective-permute-start.3
  131.8 12.5 %collective-permute-done.3 = f32[256,512]{1,0:T(8,128)S(1)} collective-permute-done((f32[256,512]{1,0:T(8,128)S(1)}, f32[256,512]{1,0:T(8,128)S(1)}, u32[]{:S(2)}, u32[]{:S(2)}) %collective-permute-start.3) | collective-permute-done | bytes 524320 | tf_op jit(solution)/shard_map/ppermute | solution.py:143
  144.4 1.1 subtract_select_fusion.12
  147.3 1.5 collective-permute-start.6
  150.2 11.8 %collective-permute-done.6 = f32[256,512]{1,0:T(8,128)S(1)} collective-permute-done((f32[256,512]{1,0:T(8,128)S(1)}, f32[256,512]{1,0:T(8,128)S(1)}, u32[]{:S(2)}, u32[]{:S(2)}) %collective-permute-start.6) | collective-permute-done | bytes 524320 | tf_op jit(solution)/shard_map/ppermute | solution.py:143
  162.8 1.1 subtract_select_fusion.6
  165.1 1.4 collective-permute-start.9
  167.5 1.2 fusion.21
  170.3 8.8 %collective-permute-done.9 = f32[256,512]{1,0:T(8,128)S(1)} collective-permute-done((f32[256,512]{1,0:T(8,128)S(1)}, f32[256,512]{1,0:T(8,128)S(1)}, u32[]{:S(2)}, u32[]{:S(2)}) %collective-permute-start.9) | collective-permute-done | bytes 524320 | tf_op jit(solution)/shard_map/ppermute | solution.py:143
  179.2 1.1 subtract_select_fusion
  181.4 1.5 collective-permute-start.12
  184.5 9.9 %collective-permute-done.12 = f32[256,512]{1,0:T(8,128)S(1)} collective-permute-done((f32[256,512]{1,0:T(8,128)S(1)}, f32[256,512]{1,0:T(8,128)S(1)}, u32[]{:S(2)}, u32[]{:S(2)}) %collective-permute-start.12) | collective-permute-done | bytes 524320 | tf_op jit(solution)/shard_map/ppermute | solution.py:143
  195.0 1.7 copy.22
  196.8 3.3 %copy.11 = f32[256,16,128]{0,1,2:T(8,128)} copy(f32[256,16,128]{2,1,0:T(8,128)} %bitcast.530) | data formatting | bytes 4194304 | tf_op jit(solution)/shard_map/reshape | solution.py:147
  200.1 3.9 %fusion = f32[256,2048]{0,1:T(8,128)} fusion(f32[256,2048]{0,1:T(8,128)} %copy.12, f32[256,16,128]{0,1,2:T(8,128)} %copy.11, f32[256,2048]{0,1:T(8,128)S(1)} %copy-done.1, f32[2048]{0:T(1024)S(1)} %copy-done.45), kind=kLoop, calls=%fused_computation.2 | loop fusion | flops 1572864 | bytes 8396800 | tf_op jit(solution)/shard_map/mul | solution.py:148
  204.0 2.9 %copy.13 = f32[256,2048]{1,0:T(8,128)} copy(f32[256,2048]{0,1:T(8,128)} %fusion) | data formatting | bytes 4194304 | tf_op jit(solution)/shard_map/mul | solution.py:148
  (185 shorter events, 39.7 us)
Async XLA Ops:
  6.5 92.2 %all-reduce.3.cloned.1.call-start = ((), (), s32[]{:S(2)}) async-start(), calls=%async_computation | async-start | bytes 1048576 | tf_op jit(solution)/shard_map/psum | solution.py:13
  8.3 41.1 %collective-permute-start = (f32[2,256,128]{2,1,0:T(8,128)}, f32[2,256,128]{2,1,0:T(8,128)}, u32[]{:S(2)}, u32[]{:S(2)}) collective-permute-start(f32[2,256,128]{2,1,0:T(8,128)} %get-tuple-element.128), channel_id=1, source_target_pairs={{0,1},{1,0},{2,3},{3,2},{4,5},{5,4},{6,7},{7,6},{8,9},{9,8},{10,11... | collective-permute-start | bytes 786440 | tf_op jit(solution)/shard_map/ppermute | solution.py:84
  17.7 45.9 %collective-permute-start.1 = (f32[256,512]{0,1:T(8,128)}, f32[256,512]{0,1:T(8,128)}, u32[]{:S(2)}, u32[]{:S(2)}) collective-permute-start(f32[256,512]{0,1:T(8,128)} %get-tuple-element.95), channel_id=1, source_target_pairs={{0,4},{4,8},{1,5},{5,9},{2,6},{6,10},{3,7},{7,11},{16,20},{20,24},... | collective-permute-start | bytes 1572872 | tf_op jit(solution)/shard_map/ppermute | solution.py:128
  19.2 33.6 %collective-permute-start.4 = (f32[256,512]{0,1:T(8,128)}, f32[256,512]{0,1:T(8,128)}, u32[]{:S(2)}, u32[]{:S(2)}) collective-permute-start(f32[256,512]{0,1:T(8,128)} %get-tuple-element.98), channel_id=1, source_target_pairs={{0,4},{4,8},{1,5},{5,9},{2,6},{6,10},{3,7},{7,11},{16,20},{20,24},... | collective-permute-start | bytes 1572872 | tf_op jit(solution)/shard_map/ppermute | solution.py:128
  20.6 35.2 %collective-permute-start.7 = (f32[256,512]{0,1:T(8,128)}, f32[256,512]{0,1:T(8,128)}, u32[]{:S(2)}, u32[]{:S(2)}) collective-permute-start(f32[256,512]{0,1:T(8,128)} %get-tuple-element.97), channel_id=1, source_target_pairs={{0,4},{4,8},{1,5},{5,9},{2,6},{6,10},{3,7},{7,11},{16,20},{20,24},... | collective-permute-start | bytes 1572872 | tf_op jit(solution)/shard_map/ppermute | solution.py:128
  22.1 38.3 %collective-permute-start.10 = (f32[256,512]{0,1:T(8,128)}, f32[256,512]{0,1:T(8,128)}, u32[]{:S(2)}, u32[]{:S(2)}) collective-permute-start(f32[256,512]{0,1:T(8,128)} %get-tuple-element.96), channel_id=1, source_target_pairs={{0,4},{4,8},{1,5},{5,9},{2,6},{6,10},{3,7},{7,11},{16,20},{20,24},... | collective-permute-start | bytes 1572872 | tf_op jit(solution)/shard_map/ppermute | solution.py:128
  28.9 3.0 %copy-start.7 = (f32[256,512]{1,0:T(8,128)}, f32[256,512]{1,0:T(8,128)S(1)}, u32[]{:S(2)}) copy-start(f32[256,512]{1,0:T(8,128)S(1)} %fusion.121) | copy-start | bytes 1572868
  29.3 2.5 %copy-start.9 = (f32[256,512]{1,0:T(8,128)}, f32[256,512]{1,0:T(8,128)S(1)}, u32[]{:S(2)}) copy-start(f32[256,512]{1,0:T(8,128)S(1)} %fusion.123) | copy-start | bytes 1572868
  29.8 3.2 %copy-start.11 = (f32[256,512]{1,0:T(8,128)}, f32[256,512]{1,0:T(8,128)S(1)}, u32[]{:S(2)}) copy-start(f32[256,512]{1,0:T(8,128)S(1)} %fusion.119) | copy-start | bytes 1572868
  30.2 2.7 %copy-start.13 = (f32[256,512]{1,0:T(8,128)}, f32[256,512]{1,0:T(8,128)S(1)}, u32[]{:S(2)}) copy-start(f32[256,512]{1,0:T(8,128)S(1)} %fusion.117) | copy-start | bytes 1572868
  30.6 3.3 %copy-start.15 = (f32[256,512]{1,0:T(8,128)}, f32[256,512]{1,0:T(8,128)S(1)}, u32[]{:S(2)}) copy-start(f32[256,512]{1,0:T(8,128)S(1)} %fusion.113) | copy-start | bytes 1572868
  31.1 2.9 %copy-start.17 = (f32[256,512]{1,0:T(8,128)}, f32[256,512]{1,0:T(8,128)S(1)}, u32[]{:S(2)}) copy-start(f32[256,512]{1,0:T(8,128)S(1)} %fusion.115) | copy-start | bytes 1572868
  54.2 6.2 %copy-start.25 = (f32[256,512]{1,0:T(8,128)}, f32[256,512]{1,0:T(8,128)S(1)}, u32[]{:S(2)}) copy-start(f32[256,512]{1,0:T(8,128)S(1)} %fusion.134) | copy-start | bytes 1572868
  55.9 4.5 %copy-start.27 = (f32[256,512]{1,0:T(8,128)}, f32[256,512]{1,0:T(8,128)S(1)}, u32[]{:S(2)}) copy-start(f32[256,512]{1,0:T(8,128)S(1)} %fusion.135) | copy-start | bytes 1572868
  57.5 7.7 %copy-start.29 = (f32[256,512]{1,0:T(8,128)}, f32[256,512]{1,0:T(8,128)S(1)}, u32[]{:S(2)}) copy-start(f32[256,512]{1,0:T(8,128)S(1)} %fusion.138) | copy-start | bytes 1572868
  59.2 6.0 %copy-start.31 = (f32[256,512]{1,0:T(8,128)}, f32[256,512]{1,0:T(8,128)S(1)}, u32[]{:S(2)}) copy-start(f32[256,512]{1,0:T(8,128)S(1)} %fusion.139) | copy-start | bytes 1572868
  61.9 5.5 %copy-start.33 = (f32[256,512]{1,0:T(8,128)}, f32[256,512]{1,0:T(8,128)S(1)}, u32[]{:S(2)}) copy-start(f32[256,512]{1,0:T(8,128)S(1)} %fusion.142) | copy-start | bytes 1572868
  63.6 3.9 %copy-start.35 = (f32[256,512]{1,0:T(8,128)}, f32[256,512]{1,0:T(8,128)S(1)}, u32[]{:S(2)}) copy-start(f32[256,512]{1,0:T(8,128)S(1)} %fusion.143) | copy-start | bytes 1572868
  63.6 54.3 %collective-permute-start.2 = (f32[256,512]{0,1:T(8,128)}, f32[256,512]{0,1:T(8,128)}, u32[]{:S(2)}, u32[]{:S(2)}) collective-permute-start(f32[256,512]{0,1:T(8,128)} %collective-permute-done.1), channel_id=1, source_target_pairs={{4,8},{5,9},{6,10},{7,11},{20,24},{21,25},{22,26},{23,27}} | collective-permute-start | bytes 1572872 | tf_op jit(solution)/shard_map/ppermute | solution.py:128
  117.8 4.0 %copy-start.19 = (f32[256,4,128]{2,1,0:T(4,128)S(1)}, f32[256,4,128]{2,1,0:T(4,128)}, u32[]{:S(2)}) copy-start(f32[256,4,128]{2,1,0:T(4,128)} %mul.550) | copy-start | bytes 1572868
  117.8 4.0 %copy-start.20 = (f32[256,4,128]{2,1,0:T(4,128)S(1)}, f32[256,4,128]{2,1,0:T(4,128)}, u32[]{:S(2)}) copy-start(f32[256,4,128]{2,1,0:T(4,128)} %mul.554) | copy-start | bytes 1572868
  117.9 13.0 %collective-permute-start.5 = (f32[256,512]{0,1:T(8,128)}, f32[256,512]{0,1:T(8,128)S(1)}, u32[]{:S(2)}, u32[]{:S(2)}) collective-permute-start(f32[256,512]{0,1:T(8,128)} %collective-permute-done.4), channel_id=1, source_target_pairs={{4,8},{5,9},{6,10},{7,11},{20,24},{21,25},{22,26},{23,27}} | collective-permute-start | bytes 1572872 | tf_op jit(solution)/shard_map/ppermute | solution.py:128
  118.7 3.6 %copy-start.44 = (f32[256,512]{1,0:T(8,128)S(1)}, f32[256,512]{1,0:T(8,128)}, u32[]{:S(2)}) copy-start(f32[256,512]{1,0:T(8,128)} %fusion.127) | copy-start | bytes 1572868
  120.2 2.1 copy-start.34
  120.2 2.1 copy-start.36
  120.3 2.1 copy-start.43
  128.8 15.6 %collective-permute-start.3 = (f32[256,512]{1,0:T(8,128)S(1)}, f32[256,512]{1,0:T(8,128)S(1)}, u32[]{:S(2)}, u32[]{:S(2)}) collective-permute-start(f32[256,512]{1,0:T(8,128)S(1)} %convolution_add_fusion.6), channel_id=1, source_target_pairs={{8,12},{9,13},{10,14},{11,15},{24,28},{25,29},{26,30},{27,31}} | collective-permute-start | bytes 1572872 | tf_op jit(solution)/shard_map/ppermute | solution.py:143
  130.8 13.5 %copy-start.2 = (f32[1,256,512]{2,1,0:T(8,128)S(1)}, f32[1,256,512]{2,1,0:T(8,128)}, u32[]{:S(2)}) copy-start(f32[1,256,512]{2,1,0:T(8,128)} %mul.583) | copy-start | bytes 1572868
  130.8 13.5 %copy-start.3 = (f32[1,256,512]{2,1,0:T(8,128)S(1)}, f32[1,256,512]{2,1,0:T(8,128)}, u32[]{:S(2)}) copy-start(f32[1,256,512]{2,1,0:T(8,128)} %mul.585) | copy-start | bytes 1572868
  130.8 13.5 %copy-start.39 = (f32[2,256,512]{2,1,0:T(8,128)S(1)}, f32[2,256,512]{2,1,0:T(8,128)}, u32[]{:S(2)}) copy-start(f32[2,256,512]{2,1,0:T(8,128)} %pad_maximum_fusion) | copy-start | bytes 3145732
  130.8 13.5 %copy-start.42 = (f32[2,256,512]{2,1,0:T(8,128)S(1)}, f32[2,256,512]{2,1,0:T(8,128)}, u32[]{:S(2)}) copy-start(f32[2,256,512]{2,1,0:T(8,128)} %pad_maximum_fusion.1) | copy-start | bytes 3145732
  146.3 3.0 %collective-permute-start.8 = (f32[256,512]{0,1:T(8,128)}, f32[256,512]{0,1:T(8,128)S(1)}, u32[]{:S(2)}, u32[]{:S(2)}) collective-permute-start(f32[256,512]{0,1:T(8,128)} %collective-permute-done.7), channel_id=1, source_target_pairs={{4,8},{5,9},{6,10},{7,11},{20,24},{21,25},{22,26},{23,27}} | collective-permute-start | bytes 1572872 | tf_op jit(solution)/shard_map/ppermute | solution.py:128
  147.3 14.7 %collective-permute-start.6 = (f32[256,512]{1,0:T(8,128)S(1)}, f32[256,512]{1,0:T(8,128)S(1)}, u32[]{:S(2)}, u32[]{:S(2)}) collective-permute-start(f32[256,512]{1,0:T(8,128)S(1)} %convolution_add_fusion.4), channel_id=1, source_target_pairs={{8,12},{9,13},{10,14},{11,15},{24,28},{25,29},{26,30},{27,31}} | collective-permute-start | bytes 1572872 | tf_op jit(solution)/shard_map/ppermute | solution.py:143
  149.3 13.5 %copy-start.38 = (f32[2,256,512]{2,1,0:T(8,128)S(1)}, f32[2,256,512]{2,1,0:T(8,128)}, u32[]{:S(2)}) copy-start(f32[2,256,512]{2,1,0:T(8,128)} %pad_maximum_fusion.3) | copy-start | bytes 3145732
  149.3 13.5 %copy-start.41 = (f32[2,256,512]{2,1,0:T(8,128)S(1)}, f32[2,256,512]{2,1,0:T(8,128)}, u32[]{:S(2)}) copy-start(f32[2,256,512]{2,1,0:T(8,128)} %pad_maximum_fusion.4) | copy-start | bytes 3145732
  162.1 4.5 %collective-permute-start.11 = (f32[256,512]{0,1:T(8,128)}, f32[256,512]{0,1:T(8,128)S(1)}, u32[]{:S(2)}, u32[]{:S(2)}) collective-permute-start(f32[256,512]{0,1:T(8,128)} %collective-permute-done.10), channel_id=1, source_target_pairs={{4,8},{5,9},{6,10},{7,11},{20,24},{21,25},{22,26},{23,27}} | collective-permute-start | bytes 1572872 | tf_op jit(solution)/shard_map/ppermute | solution.py:128
  164.7 2.8 %copy-start.8 = (f32[256,512]{1,0:T(8,128)S(1)}, f32[256,512]{1,0:T(8,128)}, u32[]{:S(2)}) copy-start(f32[256,512]{1,0:T(8,128)} %copy-done.7) | copy-start | bytes 1572868
  164.7 2.8 %copy-start.10 = (f32[256,512]{1,0:T(8,128)S(1)}, f32[256,512]{1,0:T(8,128)}, u32[]{:S(2)}) copy-start(f32[256,512]{1,0:T(8,128)} %copy-done.9) | copy-start | bytes 1572868
  164.7 2.8 %copy-start.12 = (f32[256,512]{1,0:T(8,128)S(1)}, f32[256,512]{1,0:T(8,128)}, u32[]{:S(2)}) copy-start(f32[256,512]{1,0:T(8,128)} %copy-done.11) | copy-start | bytes 1572868
  164.7 2.8 %copy-start.14 = (f32[256,512]{1,0:T(8,128)S(1)}, f32[256,512]{1,0:T(8,128)}, u32[]{:S(2)}) copy-start(f32[256,512]{1,0:T(8,128)} %copy-done.13) | copy-start | bytes 1572868
  164.7 2.8 %copy-start.16 = (f32[256,512]{1,0:T(8,128)S(1)}, f32[256,512]{1,0:T(8,128)}, u32[]{:S(2)}) copy-start(f32[256,512]{1,0:T(8,128)} %copy-done.15) | copy-start | bytes 1572868
  164.7 2.8 %copy-start.18 = (f32[256,512]{1,0:T(8,128)S(1)}, f32[256,512]{1,0:T(8,128)}, u32[]{:S(2)}) copy-start(f32[256,512]{1,0:T(8,128)} %copy-done.17) | copy-start | bytes 1572868
  165.1 14.0 %collective-permute-start.9 = (f32[256,512]{1,0:T(8,128)S(1)}, f32[256,512]{1,0:T(8,128)S(1)}, u32[]{:S(2)}, u32[]{:S(2)}) collective-permute-start(f32[256,512]{1,0:T(8,128)S(1)} %convolution_add_fusion.2), channel_id=1, source_target_pairs={{8,12},{9,13},{10,14},{11,15},{24,28},{25,29},{26,30},{27,31}} | collective-permute-start | bytes 1572872 | tf_op jit(solution)/shard_map/ppermute | solution.py:143
  169.5 9.7 %copy-start.37 = (f32[2,256,512]{2,1,0:T(8,128)S(1)}, f32[2,256,512]{2,1,0:T(8,128)}, u32[]{:S(2)}) copy-start(f32[2,256,512]{2,1,0:T(8,128)} %pad_maximum_fusion.6) | copy-start | bytes 3145732
  169.5 9.6 %copy-start.40 = (f32[2,256,512]{2,1,0:T(8,128)S(1)}, f32[2,256,512]{2,1,0:T(8,128)}, u32[]{:S(2)}) copy-start(f32[2,256,512]{2,1,0:T(8,128)} %pad_maximum_fusion.7) | copy-start | bytes 3145732
  181.4 13.0 %collective-permute-start.12 = (f32[256,512]{1,0:T(8,128)S(1)}, f32[256,512]{1,0:T(8,128)S(1)}, u32[]{:S(2)}, u32[]{:S(2)}) collective-permute-start(f32[256,512]{1,0:T(8,128)S(1)} %convolution_add_fusion), channel_id=1, source_target_pairs={{8,12},{9,13},{10,14},{11,15},{24,28},{25,29},{26,30},{27,31}} | collective-permute-start | bytes 1572872 | tf_op jit(solution)/shard_map/ppermute | solution.py:143
  196.8 3.4 %copy-start.1 = (f32[256,2048]{0,1:T(8,128)S(1)}, f32[256,2048]{0,1:T(8,128)}, u32[]{:S(2)}) copy-start(f32[256,2048]{0,1:T(8,128)} %copy-done) | copy-start | bytes 6291460
  196.8 3.4 %copy-start.45 = (f32[2048]{0:T(1024)S(1)}, f32[2048]{0:T(1024)}, u32[]{:S(2)}) copy-start(f32[2048]{0:T(1024)} %param.9) | copy-start | bytes 24580
  (13 other events, 17.6 us)
Sparse Core Ops, SparseCore 0:
  52.8 45.8 all-reduce.2
where the time goes:
time: 218 us; the launch traced here: 214 us
  waiting for transfers between devices  72.2 us (33%)
  local copies, waits for them, and re-layouts  39.8 us (18%)
  matrix products  33.5 us (15%)
  other arithmetic  27.5 us (13%)
  between operations  25.1 us (12%)
  starting transfers between devices  15.9 us (7%)
    ppermute x4, waiting for transfers between devices, body(): sent = lax.ppermute(partial, 'ctx', [(last_raw, last_raw + 1)])  43.1 us
    psum x1, waiting for transfers between devices, from_root(): return lax.psum(block, axis)  29 us
    unnamed x101, local copies, waits for them, and re-layouts  15.8 us
    dot_general x13, matrix products, transform(): jnp.dot(fwd_imag, block, precision=precision)  14.5 us
    dot_general x13, matrix products, transform(): jnp.dot(fwd_real, block, precision=precision)  12.8 us
    ppermute x8, starting transfers between devices, body(): moving = lax.ppermute(moving, 'ctx', route)  10.2 us
    another operation x9, other arithmetic, transform(): jnp.stack([jnp.dot(fwd_real, block, precision=precision), jnp.dot(fwd_ima...  6.78 us
    mul x10, local copies, waits for them, and re-layouts, apply_filter(): a_real * e_real  6.2 us
  transfers between devices with their start and end apart: 14, of which 5 were waited for; matrix products, arithmetic and copies ran while one was open for 37% of the time, Pallas kernels for 0%

commit v1 on v0

--- a/solution.py
+++ b/solution.py
@@ -5,7 +5,7 @@
 
 HIGHEST = lax.Precision.HIGHEST
 DATA_PRECISION = lax.Precision.HIGH
-CHUNKS = 4
+CHUNKS = 2
 
 
 def from_root(block, axis, owner):

time: 218 us -> 223 us (1.023); the launches traced: 214 us -> 222 us
  waiting for transfers between devices: 72.2 us -> 78.7 us
  starting transfers between devices: 15.9 us -> 9.59 us
  local copies, waits for them, and re-layouts: 39.8 us -> 43.9 us
  matrix products: 33.5 us -> 36.1 us
    psum x1, waiting for transfers between devices: 29 us -> 42.1 us  [from_root(): return lax.psum(block, axis)]
    ppermute x4 -> x2, waiting for transfers between devices: 43.1 us -> 36.5 us  [body(): sent = lax.ppermute(partial, 'ctx', [(last_raw, last_raw + 1)])]
    dot_general x13 -> x7, matrix products: 12.8 us -> 18.2 us  [transform(): jnp.dot(fwd_real, block, precision=precision)]
    add x8 -> x4, other arithmetic: 2.79 us -> 7.03 us  [filtered_sum(): total = total + apply_filter(spec, filt)]
    ppermute x8 -> x4, starting transfers between devices: 10.2 us -> 6.65 us  [body(): moving = lax.ppermute(moving, 'ctx', route)]
    another operation x9 -> x3, other arithmetic: 6.78 us -> 3.49 us  [transform(): jnp.stack([jnp.dot(fwd_real, block, precision=precision), jnp.dot(fwd_ima...]
    mul x8, local copies, waits for them, and re-layouts: 5.52 us -> 8.59 us  [apply_filter(): a_imag * e_imag]
    mul x10, local copies, waits for them, and re-layouts: 6.2 us -> 9.27 us  [apply_filter(): a_real * e_real]
  transfers between devices with their start and end apart: 14 -> 8, of which waited for: 5 -> 3; matrix products, arithmetic and copies ran while one was open for 37% -> 38% of each run, Pallas kernels for 0% -> 0%
where the time goes in v1:
time: 223 us; the launch traced here: 222 us
  waiting for transfers between devices  78.7 us (35%)
  local copies, waits for them, and re-layouts  43.9 us (20%)
  matrix products  36.1 us (16%)
  other arithmetic  29.6 us (13%)
  between operations  24.2 us (11%)
  starting transfers between devices  9.59 us (4%)
    psum x1, waiting for transfers between devices, from_root(): return lax.psum(block, axis)  42.1 us
    ppermute x2, waiting for transfers between devices, body(): sent = lax.ppermute(partial, 'ctx', [(last_raw, last_raw + 1)])  36.5 us
    dot_general x7, matrix products, transform(): jnp.dot(fwd_real, block, precision=precision)  18.2 us
    unnamed x57, local copies, waits for them, and re-layouts  13.8 us
    dot_general x7, matrix products, transform(): jnp.dot(fwd_imag, block, precision=precision)  11.5 us
    mul x10, local copies, waits for them, and re-layouts, apply_filter(): a_real * e_real  9.27 us
    mul x8, local copies, waits for them, and re-layouts, apply_filter(): a_imag * e_imag  8.59 us
    add x4, other arithmetic, filtered_sum(): total = total + apply_filter(spec, filt)  7.03 us
  transfers between devices with their start and end apart: 8, of which 3 were waited for; matrix products, arithmetic and copies ran while one was open for 38% of the time, Pallas kernels for 0%

profile of v1, /device:TPU:24, one launch (start us, length us, event | category | flops | bytes accessed | tf_op | source)
XLA Modules:
  0.0 222.1 jit_solution(397522761952896602)
XLA Ops:
  6.5 1.8 constant_dynamic-slice_fusion
  8.3 1.9 copy.8
  10.2 2.9 %copy.9 = f32[256,2048]{0,1:T(8,128)} copy(f32[256,2048]{1,0:T(8,128)} %param.8) | data formatting | bytes 4194304 | tf_op args[2]
  13.1 1.9 mul.321
  15.0 1.2 copy.10
  16.3 1.5 fusion.87
  17.8 1.6 collective-permute-start.1
  19.5 1.7 collective-permute-start.4
  33.1 2.1 select_multiply_fusion
  35.2 1.7 fusion.79
  36.9 1.6 fusion.81
  38.5 2.9 %copy.12 = f32[256,2048]{0,1:T(8,128)} copy(f32[256,2048]{1,0:T(8,128)} %param.6) | data formatting | bytes 4194304 | tf_op args[0]
  41.4 3.1 %pad_maximum_fusion = f32[2,256,1024]{2,1,0:T(8,128)} fusion(f32[1,256,1024]{2,1,0:T(8,128)} %bitcast.338, f32[1,256,1024]{2,1,0:T(8,128)} %bitcast.339), kind=kLoop, calls=%fused_computation.6 | loop fusion | flops 524288 | bytes 4194304 | tf_op jit(solution)/shard_map/stack | solution.py:32
  44.5 1.6 fusion.75
  46.1 1.7 fusion.66
  47.8 1.6 fusion.83
  49.4 1.6 fusion.85
  51.0 42.1 %all-reduce.3.cloned.1.call-done = (f32[256,128]{1,0:T(8,128)}, f32[256,128]{1,0:T(8,128)}, f32[256,128]{1,0:T(8,128)}, f32[256,128]{1,0:T(8,128)}) async-done(((f32[256,128]{1,0:T(8,128)}, f32[256,128]{1,0:T(8,128)}, f32[256,128]{1,0:T(8,128)}, f32[256,128]{1,0:T(8,128)}), (f32[256,128]{1,0:T(8,128)}, f32[256,128]{1,0:T(8,128)}, f32[256,128]{1,0:T(8,128)}, ...) | async-done | bytes 524304 | tf_op jit(solution)/shard_map/psum | solution.py:13
  99.6 1.6 collective-permute-start.2
  102.0 1.3 mul.714
  104.3 1.3 mul.716
  106.5 1.1 mul.720
  107.7 1.1 mul.722
  108.9 2.0 mul.693
  110.9 2.4 %mul.726 = f32[1,256,1024]{2,1,0:T(8,128)} reshape(f32[256,8,128]{2,1,0:T(8,128)} %mul.693) | data formatting | bytes 2097152 | tf_op jit(solution)/shard_map/mul | solution.py:52
  114.3 2.4 %mul.728 = f32[1,256,1024]{2,1,0:T(8,128)} reshape(f32[256,8,128]{2,1,0:T(8,128)} %mul.697) | data formatting | bytes 2097152 | tf_op jit(solution)/shard_map/mul | solution.py:52
  116.7 1.8 fusion.92
  118.5 1.8 fusion.93
  120.6 2.0 fusion.89
  122.6 1.7 collective-permute-start.5
  124.3 2.0 fusion.90
  126.4 2.0 fusion.91
  129.6 8.7 %fusion.8 = (f32[1,256,1024]{2,1,0:T(8,128)}, f32[1,256,1024]{2,1,0:T(8,128)}, f32[1,256,1024]{2,1,0:T(8,128)}, f32[1,256,1024]{2,1,0:T(8,128)}, f32[1,256,1024]...) fusion(f32[256,1024]{1,0:T(8,128)S(1)} %fusion.89, ...), kind=kOutput, calls=%fused_computation.41 | convolution fusion | flops 417333248 | bytes 33816832 | tf_op jit(solution)/shard_map/dot_general | solution.py:33
  138.3 3.5 %fusion.1 = f32[2,256,1024]{2,1,0:T(8,128)S(1)} fusion(f32[1,256,1024]{2,1,0:T(8,128)} %get-tuple-element.55, f32[1,256,1024]{2,1,0:T(8,128)} %get-tuple-element.56, f32[1,256,1024]{2,1,0:T(8,128)} %get-tuple-element.61, f32[1,256,1024]{2,1,0:T(8,128)} %get-tuple-element.62, f32[1,256,1024]{2,1,0:T(8,128)} %get-tuple-element.84, ...), kind=kLoop, calls=%fused_computation.3 | loop fusion | flops 2621440 | bytes 8388608 | tf_op jit(solution)/shard_map/add | solution.py:60
  143.1 1.5 collective-permute-start.3
  144.6 1.8 fusion.94
  146.5 1.8 fusion.95
  148.5 1.2 fusion.9
  149.7 19.1 %collective-permute-done.3 = f32[256,1024]{1,0:T(8,128)} collective-permute-done((f32[256,1024]{1,0:T(8,128)S(1)}, f32[256,1024]{1,0:T(8,128)}, u32[]{:S(2)}, u32[]{:S(2)}) %collective-permute-start.3) | collective-permute-done | bytes 1048608 | tf_op jit(solution)/shard_map/ppermute | solution.py:143
  168.8 5.5 %subtract_select_fusion = (f32[1,256,1024]{2,1,0:T(8,128)S(1)}, f32[1,256,1024]{2,1,0:T(8,128)S(1)}, f32[1,256,1024]{2,1,0:T(8,128)S(1)}, f32[1,256,1024]{2,1,0:...) fusion(f32[1,256,1024]{2,1,0:T(8,128)} %mul.726, f32[2,256,1024]{2,1,0:T(8,128)S(1)} %pad_maximum_fusion.2, ...), kind=kLoop, calls=%fused_computation.14 | loop fusion | flops 6291456 | bytes 18874624 | tf_op jit(solution)/shard_map/jit(_where)/select_n | solution.py:52
  174.2 2.2 fusion.3
  177.7 1.4 collective-permute-start.6
  183.3 1.9 fusion.6
  185.2 17.4 %collective-permute-done.6 = f32[256,1024]{1,0:T(8,128)S(1)} collective-permute-done((f32[256,1024]{1,0:T(8,128)S(1)}, f32[256,1024]{1,0:T(8,128)S(1)}, u32[]{:S(2)}, u32[]{:S(2)}) %collective-permute-start.6) | collective-permute-done | bytes 1048608 | tf_op jit(solution)/shard_map/ppermute | solution.py:143
  203.4 1.7 copy.22
  205.1 3.3 %copy.11 = f32[256,16,128]{0,1,2:T(8,128)} copy(f32[256,16,128]{2,1,0:T(8,128)} %bitcast.344) | data formatting | bytes 4194304 | tf_op jit(solution)/shard_map/reshape | solution.py:147
  208.4 3.9 %fusion.4 = f32[256,2048]{0,1:T(8,128)} fusion(f32[256,2048]{0,1:T(8,128)} %copy.12, f32[256,16,128]{0,1,2:T(8,128)} %copy.11, f32[256,2048]{0,1:T(8,128)S(1)} %copy-done.1, f32[2048]{0:T(1024)S(1)} %copy-done.23), kind=kLoop, calls=%fused_computation.13 | loop fusion | flops 1572864 | bytes 8396800 | tf_op jit(solution)/shard_map/mul | solution.py:148
  212.4 2.9 %copy.13 = f32[256,2048]{1,0:T(8,128)} copy(f32[256,2048]{0,1:T(8,128)} %fusion.4) | data formatting | bytes 4194304 | tf_op jit(solution)/shard_map/mul | solution.py:148
  (96 shorter events, 21.0 us)
Async XLA Ops:
  6.5 86.6 %all-reduce.3.cloned.1.call-start = ((), (), s32[]{:S(2)}) async-start(), calls=%async_computation | async-start | bytes 1048576 | tf_op jit(solution)/shard_map/psum | solution.py:13
  8.3 36.2 %collective-permute-start = (f32[2,256,128]{2,1,0:T(8,128)}, f32[2,256,128]{2,1,0:T(8,128)}, u32[]{:S(2)}, u32[]{:S(2)}) collective-permute-start(f32[2,256,128]{2,1,0:T(8,128)} %get-tuple-element.72), channel_id=1, source_target_pairs={{0,1},{1,0},{2,3},{3,2},{4,5},{5,4},{6,7},{7,6},{8,9},{9,8},{10,11... | collective-permute-start | bytes 786440 | tf_op jit(solution)/shard_map/ppermute | solution.py:84
  15.0 1.3 copy-start
  16.3 4.8 %copy-start.24 = (s32[4]{0:T(128)S(1)}, s32[4]{0:T(128)}, u32[]{:S(2)}) copy-start(s32[4]{0:T(128)} %param.11) | copy-start | bytes 52
  17.8 81.7 %collective-permute-start.1 = (f32[256,1024]{0,1:T(8,128)}, f32[256,1024]{0,1:T(8,128)}, u32[]{:S(2)}, u32[]{:S(2)}) collective-permute-start(f32[256,1024]{0,1:T(8,128)} %get-tuple-element.63), channel_id=1, source_target_pairs={{0,4},{4,8},{1,5},{5,9},{2,6},{6,10},{3,7},{7,11},{16,20},{20,24},... | collective-permute-start | bytes 3145736 | tf_op jit(solution)/shard_map/ppermute | solution.py:128
  19.5 97.2 %collective-permute-start.4 = (f32[256,1024]{0,1:T(8,128)}, f32[256,1024]{0,1:T(8,128)}, u32[]{:S(2)}, u32[]{:S(2)}) collective-permute-start(f32[256,1024]{0,1:T(8,128)} %get-tuple-element.64), channel_id=1, source_target_pairs={{0,4},{4,8},{1,5},{5,9},{2,6},{6,10},{3,7},{7,11},{16,20},{20,24},... | collective-permute-start | bytes 3145736 | tf_op jit(solution)/shard_map/ppermute | solution.py:128
  99.6 23.0 %collective-permute-start.2 = (f32[256,1024]{0,1:T(8,128)}, f32[256,1024]{0,1:T(8,128)}, u32[]{:S(2)}, u32[]{:S(2)}) collective-permute-start(f32[256,1024]{0,1:T(8,128)} %collective-permute-done.1), channel_id=1, source_target_pairs={{4,8},{5,9},{6,10},{7,11},{20,24},{21,25},{22,26},{23,27}} | collective-permute-start | bytes 3145736 | tf_op jit(solution)/shard_map/ppermute | solution.py:128
  102.0 3.5 %copy-start.2 = (f32[256,8,128]{2,1,0:T(8,128)}, f32[256,8,128]{2,1,0:T(8,128)S(1)}, u32[]{:S(2)}) copy-start(f32[256,8,128]{2,1,0:T(8,128)S(1)} %mul.663) | copy-start | bytes 3145732
  104.3 3.4 %copy-start.4 = (f32[256,8,128]{2,1,0:T(8,128)}, f32[256,8,128]{2,1,0:T(8,128)S(1)}, u32[]{:S(2)}) copy-start(f32[256,8,128]{2,1,0:T(8,128)S(1)} %mul.667) | copy-start | bytes 3145732
  108.9 4.4 %copy-start.22 = (f32[256,128]{1,0:T(8,128)S(1)}, f32[256,128]{1,0:T(8,128)}, u32[]{:S(2)}) copy-start(f32[256,128]{1,0:T(8,128)} %get-tuple-element.77) | copy-start | bytes 393220
  120.6 8.9 %copy-start.11 = (f32[256,1024]{1,0:T(8,128)S(1)}, f32[256,1024]{1,0:T(8,128)}, u32[]{:S(2)}) copy-start(f32[256,1024]{1,0:T(8,128)} %fusion.83) | copy-start | bytes 3145732
  120.6 8.9 %copy-start.12 = (f32[256,1024]{1,0:T(8,128)S(1)}, f32[256,1024]{1,0:T(8,128)}, u32[]{:S(2)}) copy-start(f32[256,1024]{1,0:T(8,128)} %fusion.85) | copy-start | bytes 3145732
  122.6 22.0 %collective-permute-start.5 = (f32[256,1024]{0,1:T(8,128)}, f32[256,1024]{0,1:T(8,128)}, u32[]{:S(2)}, u32[]{:S(2)}) collective-permute-start(f32[256,1024]{0,1:T(8,128)} %collective-permute-done.4), channel_id=1, source_target_pairs={{4,8},{5,9},{6,10},{7,11},{20,24},{21,25},{22,26},{23,27}} | collective-permute-start | bytes 3145736 | tf_op jit(solution)/shard_map/ppermute | solution.py:128
  124.3 5.2 %copy-start.8 = (f32[256,1024]{1,0:T(8,128)S(1)}, f32[256,1024]{1,0:T(8,128)}, u32[]{:S(2)}) copy-start(f32[256,1024]{1,0:T(8,128)} %fusion.79) | copy-start | bytes 3145732
  124.3 5.2 %copy-start.9 = (f32[256,1024]{1,0:T(8,128)S(1)}, f32[256,1024]{1,0:T(8,128)}, u32[]{:S(2)}) copy-start(f32[256,1024]{1,0:T(8,128)} %fusion.81) | copy-start | bytes 3145732
  126.3 3.2 %copy-start.3 = (f32[256,8,128]{2,1,0:T(8,128)S(1)}, f32[256,8,128]{2,1,0:T(8,128)}, u32[]{:S(2)}) copy-start(f32[256,8,128]{2,1,0:T(8,128)} %copy-done.2) | copy-start | bytes 3145732
  126.3 3.2 %copy-start.5 = (f32[256,8,128]{2,1,0:T(8,128)S(1)}, f32[256,8,128]{2,1,0:T(8,128)}, u32[]{:S(2)}) copy-start(f32[256,8,128]{2,1,0:T(8,128)} %copy-done.4) | copy-start | bytes 3145732
  126.3 3.2 %copy-start.6 = (f32[256,8,128]{2,1,0:T(8,128)S(1)}, f32[256,8,128]{2,1,0:T(8,128)}, u32[]{:S(2)}) copy-start(f32[256,8,128]{2,1,0:T(8,128)} %mul.693) | copy-start | bytes 3145732
  126.4 3.2 %copy-start.7 = (f32[256,8,128]{2,1,0:T(8,128)S(1)}, f32[256,8,128]{2,1,0:T(8,128)}, u32[]{:S(2)}) copy-start(f32[256,8,128]{2,1,0:T(8,128)} %mul.697) | copy-start | bytes 3145732
  143.1 25.7 %collective-permute-start.3 = (f32[256,1024]{1,0:T(8,128)S(1)}, f32[256,1024]{1,0:T(8,128)}, u32[]{:S(2)}, u32[]{:S(2)}) collective-permute-start(f32[256,1024]{1,0:T(8,128)S(1)} %convolution_add_fusion.2), channel_id=1, source_target_pairs={{8,12},{9,13},{10,14},{11,15},{24,28},{25,29},{26,30},{27,31}} | collective-permute-start | bytes 3145736 | tf_op jit(solution)/shard_map/ppermute | solution.py:143
  148.4 20.3 %copy-start.10 = (f32[2,256,1024]{2,1,0:T(8,128)S(1)}, f32[2,256,1024]{2,1,0:T(8,128)}, u32[]{:S(2)}) copy-start(f32[2,256,1024]{2,1,0:T(8,128)} %pad_maximum_fusion) | copy-start | bytes 6291460
  148.5 20.3 %copy-start.21 = (f32[1,256,1024]{2,1,0:T(8,128)S(1)}, f32[1,256,1024]{2,1,0:T(8,128)}, u32[]{:S(2)}) copy-start(f32[1,256,1024]{2,1,0:T(8,128)} %mul.714) | copy-start | bytes 3145732
  176.4 2.7 %copy-start.20 = (f32[1,256,1024]{2,1,0:T(8,128)S(1)}, f32[1,256,1024]{2,1,0:T(8,128)}, u32[]{:S(2)}) copy-start(f32[1,256,1024]{2,1,0:T(8,128)} %get-tuple-element.58) | copy-start | bytes 3145732
  177.1 2.1 copy-start.17
  177.1 2.1 copy-start.18
  177.1 2.1 copy-start.19
  177.7 24.8 %collective-permute-start.6 = (f32[256,1024]{1,0:T(8,128)S(1)}, f32[256,1024]{1,0:T(8,128)S(1)}, u32[]{:S(2)}, u32[]{:S(2)}) collective-permute-start(f32[256,1024]{1,0:T(8,128)S(1)} %convolution_add_fusion), channel_id=1, source_target_pairs={{8,12},{9,13},{10,14},{11,15},{24,28},{25,29},{26,30},{27,31}} | collective-permute-start | bytes 3145736 | tf_op jit(solution)/shard_map/ppermute | solution.py:143
  179.2 1.2 copy-start.13
  179.2 1.5 copy-start.14
  179.2 1.8 copy-start.15
  179.2 2.1 copy-start.16
  205.1 3.3 %copy-start.1 = (f32[256,2048]{0,1:T(8,128)S(1)}, f32[256,2048]{0,1:T(8,128)}, u32[]{:S(2)}) copy-start(f32[256,2048]{0,1:T(8,128)} %copy-done) | copy-start | bytes 6291460
  205.1 3.3 %copy-start.23 = (f32[2048]{0:T(1024)S(1)}, f32[2048]{0:T(1024)}, u32[]{:S(2)}) copy-start(f32[2048]{0:T(1024)} %param.9) | copy-start | bytes 24580
Sparse Core Ops, SparseCore 0:
  47.9 45.1 all-reduce.2
